TPU v7x, 512 devices: a whole 4x8x8 slice. The times are simulated.
512 devices in a mesh: rx: 8 (over y), tm: 16 (over z, core), bin: 4 (over x).
Axes of the slice: x: 4, y: 8, z: 8, core: 2. Of those that a mesh axis runs over, the one named last changes fastest.
Arguments:
- samples: bfloat16 [4, 4096, 4096], P('bin', 'tm', 'rx'), may hold values from -45 to 45, as said below
- test_matrix: bfloat16 [4, 4096, 512], P('bin', 'tm'), may hold values from -0.09375 to 0.09375
- forgetting: float32 [4, 16, 512], P('bin', 'tm'), may hold values from 0 to 1, as said below
- prior_sketch: bfloat16 [4, 4096, 512], P('bin', 'rx'), may hold values from -6 to 6
Outputs:
- basis: bfloat16 [4, 16, 4096, 512], P('bin', 'tm', 'rx')
- coefficients: float32 [4, 4096, 512], P('bin', 'tm')
Inputs may be any that keep to these rules, and one draw needn't show every extreme that they name: `samples`: real-valued data. `forgetting`: positive factors.
All inputs are finite; a program needn't handle non-finite values.
Results may differ from a plain program's by a relative error of at most 0.015.
Values may be sent and summed in bfloat16 or wider, within the bound.
No kernel may reach another device: no remote copies, remote signals or barrier semaphores. Data moves between devices by JAX's collectives and lax.ppermute only.
A program may use at most 64 MiB of HBM per device.

v0:
```python
import math
import jax
import jax.numpy as jnp
from jax import lax
from jax.sharding import PartitionSpec as P


def prefix_2(part, axis, combine, identity):
    place = lax.axis_index(axis)
    gathered = jax.tree.map(lambda a: lax.all_gather(a, axis), part)
    state = jax.tree.map(lambda a, e: jnp.zeros_like(a) + jnp.asarray(e, a.dtype), part, identity)

    def one(hop, state):
        return combine(
            state, jax.tree.map(lambda a: lax.dynamic_index_in_dim(a, hop, 0, False), gathered)
        )

    return lax.fori_loop(0, place, one, state)


def with_halo(block, sides, width):
    for axis, dim in sides:
        count = lax.axis_size(axis)
        forward = [(i, i + 1) for i in range(count - 1)]
        backward = [(target, source) for source, target in forward]
        low = lax.ppermute(
            lax.slice_in_dim(block, block.shape[dim] - width, None, axis=dim), axis, forward
        )
        high = lax.ppermute(lax.slice_in_dim(block, 0, width, axis=dim), axis, backward)
        block = jnp.concatenate([low, block, high], axis=dim)
    return block


def combine(earlier, later):
    return (earlier[0] * later[0], later[0][None, :] * earlier[1] + later[1])


def sketch_of(block_data, block_test):
    return lax.dot_general(
        block_data, block_test, (((0,), (0,)), ((), ())), preferred_element_type=jnp.float32
    )


def body(samples, test_matrix, forgetting, prior_sketch):
    block_data = samples[0]
    block_test = test_matrix[0]
    own_decay = forgetting[0, 0]
    prior_rows = prior_sketch[0].astype(jnp.float32)
    width = block_test.shape[1]
    rows = block_data.shape[1]
    sketch = sketch_of(block_data, block_test)
    identity = (jnp.ones((width,), jnp.float32), jnp.zeros((rows, width), jnp.float32))
    before_decay, before_sum = prefix_2((own_decay, sketch), "tm", combine, identity)
    prefix = (
        own_decay[None, :] * before_sum + sketch + (before_decay * own_decay)[None, :] * prior_rows
    )
    padded = with_halo(prefix[None], (("bin", 0),), 1)
    mixed = padded[1] + 0.25 * (padded[0] + padded[2])
    local_gram = lax.dot_general(
        mixed,
        mixed,
        (((0,), (0,)), ((), ())),
        precision=lax.Precision.HIGHEST,
        preferred_element_type=jnp.float32,
    )
    gram = lax.psum(local_gram, "rx")
    factor = jnp.linalg.cholesky(gram)
    ortho = jax.scipy.linalg.solve_triangular(factor, mixed.T, lower=True).T
    local_coords = jnp.dot(
        block_data.astype(jnp.float32),
        ortho,
        precision=lax.Precision.HIGHEST,
        preferred_element_type=jnp.float32,
    )
    coords = lax.psum(local_coords.astype(jnp.bfloat16), "rx").astype(jnp.float32)
    receivers = rows * lax.axis_size("rx")
    basis = (math.sqrt(receivers) * ortho).astype(jnp.bfloat16)
    return (basis[None, None], coords[None])


def solution(mesh):
    return jax.shard_map(
        body,
        mesh=mesh,
        in_specs=(
            P("bin", "tm", "rx"),
            P("bin", "tm", None),
            P("bin", "tm", None),
            P("bin", "rx", None),
        ),
        out_specs=(P("bin", "tm", "rx", None), P("bin", "tm", None)),
        check_vma=False,
    )
```

profile of v0, /device:TPU:2, one launch (start us, length us, event | category | flops | bytes accessed | tf_op | source)
XLA Modules:
  0.0 489.7 jit_solution(11235781154400756800)
XLA Ops:
  7.2 0.9 copy-done
  8.1 2.3 fusion.15
  10.5 23.6 %all-gather = f32[16,1,512]{2,1,0:T(1,128)S(1)} all-gather(f32[1,1,512]{2,1,0:T(1,128)} %param.8), channel_id=2, replica_groups=mesh['rx'=8,'tm'=16,'bin'=4] {'tm'}, dimensions={0}, use_global_device_ids=true | all-gather | bytes 34816 | tf_op jit(solution)/shard_map/all_gather | solution.py:10
  34.1 79.9 %all-gather.4.cloned.1.call-done = f32[8192,512]{1,0:T(8,128)} async-done(((f32[512,512]{1,0:T(8,128)}), f32[8192,512]{1,0:T(8,128)}) %all-gather.4.cloned.1.call-update) | async-done | bytes 16777232 | tf_op jit(solution)/shard_map/all_gather | solution.py:10
  114.5 3.4 collective-permute-start
  117.9 2.5 collective-permute-start.1
  120.4 21.0 %collective-permute-done = f32[1,512,512]{2,1,0:T(8,128)S(1)} collective-permute-done((f32[1,512,512]{2,1,0:T(8,128)S(1)}, f32[1,512,512]{2,1,0:T(8,128)S(1)}, u32[]{:S(2)}, u32[]{:S(2)}) %collective-permute-start) | collective-permute-done | bytes 1048608 | tf_op jit(solution)/shard_map/ppermute | solution.py:26
  141.4 3.7 collective-permute-done.1
  145.1 1.6 bitcast_add_fusion.2
  146.7 2.9 fusion.40
  149.6 0.5 all-reduce.6.cloned.1.call-start
  150.1 101.0 %all-reduce.4.cloned.1.call-done = f32[512,512]{0,1:T(8,128)} async-done(((f32[512,512]{0,1:T(8,128)}), f32[512,512]{0,1:T(8,128)}) %all-reduce.4.cloned.1.call-update) | async-done | bytes 1048592 | tf_op jit(solution)/shard_map/psum | solution.py:66
  251.1 1.6 copy.12
  252.7 1.4 fusion.2
  254.2 11.7 %cholesky.103 = f32[128,128]{1,0:T(8,128)S(1)} custom-call(f32[128,128]{1,0:T(8,128)S(1)} %cholesky.263), custom_call_target="Cholesky" | custom-call | tf_op jit(solution)/shard_map/jit(cholesky)/cholesky | solution.py:67
  266.0 9.8 %custom-call.31 = f32[1,128,128]{1,2,0:T(8,128)S(1)} custom-call(f32[1,128,128]{2,1,0:T(8,128)S(1)} %get-tuple-element.81), custom_call_target="InvertDiagBlocksLowerTriangular" | custom-call | tf_op jit(solution)/shard_map/jit(cholesky)/cholesky | solution.py:67
  276.5 0.7 copy-done.3
  277.2 11.7 %cholesky.215 = f32[128,128]{1,0:T(8,128)S(1)} custom-call(f32[128,128]{1,0:T(8,128)S(1)} %cholesky.267), custom_call_target="Cholesky" | custom-call | tf_op jit(solution)/shard_map/jit(cholesky)/cholesky | solution.py:67
  288.9 10.0 %custom-call.32 = f32[1,128,128]{1,2,0:T(8,128)S(1)} custom-call(f32[1,128,128]{2,1,0:T(8,128)S(1)} %get-tuple-element.78), custom_call_target="InvertDiagBlocksLowerTriangular" | custom-call | tf_op jit(solution)/shard_map/jit(cholesky)/cholesky | solution.py:67
  298.9 1.2 convolution_dynamic-update-slice_fusion
  300.5 0.6 cholesky.272
  301.1 13.2 %cholesky.236 = f32[128,128]{1,0:T(8,128)} custom-call(f32[128,128]{1,0:T(8,128)} %cholesky.272), custom_call_target="Cholesky" | custom-call | tf_op jit(solution)/shard_map/jit(cholesky)/cholesky | solution.py:67
  314.3 1.5 select_reduce_fusion.1
  315.8 0.7 compare_reduce_fusion.1
  316.4 11.3 %custom-call.33 = f32[1,128,128]{1,2,0:T(8,128)} custom-call(f32[1,128,128]{2,1,0:T(8,128)} %get-tuple-element.75), custom_call_target="InvertDiagBlocksLowerTriangular" | custom-call | tf_op jit(solution)/shard_map/jit(cholesky)/cholesky | solution.py:67
  327.7 1.0 convolution_dynamic-update-slice_fusion.1
  329.1 11.7 %cholesky.253 = f32[128,128]{1,0:T(8,128)S(1)} custom-call(f32[128,128]{1,0:T(8,128)S(1)} %convolution_subtract_fusion.5), custom_call_target="Cholesky" | custom-call | tf_op jit(solution)/shard_map/jit(cholesky)/cholesky | solution.py:67
  340.9 0.7 compare_reduce_fusion
  341.6 0.6 compare_reduce_fusion.2
  345.1 10.9 %while.14 = (s32[]{:T(128)}, f32[512,512]{1,0:T(8,128)S(1)}, s32[4,2]{0,1:T(2,128)S(1)}, f32[4,128,128]{2,1,0:T(8,128)}, s32[]{:T(128)}) while((s32[]{:T(128)}, f32[512,512]{1,0:T(8,128)S(1)}, s32[4,2]{0,1:T(2,128)S(1)}, f32[4,128,128]{2,1,0:T(8,128)}, s32[]{:T(128)}) %tuple.49), condition=%wide.while_cond, body=%wide.while_body.sunk | while | flops 2 | bytes 132705 | solution.py:68
  345.2 0.6 fusion.49
  345.8 2.1 bitcast_dynamic-update-slice_fusion.2
  347.9 0.6 fusion.49
  348.5 2.1 bitcast_dynamic-update-slice_fusion.2
  350.6 0.6 fusion.49
  351.2 2.1 bitcast_dynamic-update-slice_fusion.2
  353.4 0.6 fusion.49
  354.0 2.1 bitcast_dynamic-update-slice_fusion.2
  356.0 40.1 %custom-call.34 = f32[4,128,128]{1,2,0:T(8,128)S(1)} custom-call(f32[4,128,128]{2,1,0:T(8,128)} %get-tuple-element.45), custom_call_target="InvertDiagBlocksLowerTriangular" | custom-call | tf_op jit(solution)/shard_map/jit(_solve_triangular)/triangular_solve | solution.py:68
  396.6 0.6 convolution_subtract_fusion.1
  397.6 1.0 convolution_subtract_fusion
  398.6 1.3 fusion.27
  399.9 1.5 convolution_subtract_fusion.2
  401.4 1.3 fusion.26
  402.6 1.3 fusion
  404.1 1.0 copy.13
  405.1 75.9 %all-reduce.6.cloned.1.call-done = bf16[1,256,512]{1,2,0:T(8,128)(2,1)} async-done(((bf16[1,256,512]{1,2,0:T(8,128)(2,1)}), bf16[1,256,512]{1,2,0:T(8,128)(2,1)}) %all-reduce.6.cloned.1.call-update) | async-done | bytes 262160 | tf_op jit(solution)/shard_map/psum | solution.py:75
  481.0 1.9 copy.14
  (42 shorter events, 3.8 us)
Async XLA Ops:
  7.2 1.0 copy-start
  7.2 107.0 %copy-start.5 = (f32[1,1,512]{2,1,0:T(1,128)S(1)}, f32[1,1,512]{2,1,0:T(1,128)}, u32[]{:S(2)}) copy-start(f32[1,1,512]{2,1,0:T(1,128)} %param.8) | copy-start | bytes 6148
  7.2 107.0 %copy-start.2 = (bf16[1,512,512]{2,1,0:T(8,128)(2,1)S(1)}, bf16[1,512,512]{2,1,0:T(8,128)(2,1)}, u32[]{:S(2)}) copy-start(bf16[1,512,512]{2,1,0:T(8,128)(2,1)} %param.9) | copy-start | bytes 1572868
  7.2 106.8 %all-gather.4.cloned.1.call-start = ((), (), s32[]{:S(2)}) async-start(), calls=%async_computation.2 | async-start | bytes 17825792 | tf_op jit(solution)/shard_map/all_gather | solution.py:10
  10.4 103.8 %copy-start.1 = (f32[512,512]{1,0:T(8,128)S(1)}, f32[512,512]{1,0:T(8,128)}, u32[]{:S(2)}) copy-start(f32[512,512]{1,0:T(8,128)} %fusion.15) | copy-start | bytes 3145732
  10.4 240.7 %all-reduce.4.cloned.1.call-start = ((), (), s32[]{:S(2)}) async-start(), calls=%async_computation | async-start | bytes 2097152 | tf_op jit(solution)/shard_map/psum | solution.py:66
  114.5 27.0 %collective-permute-start = (f32[1,512,512]{2,1,0:T(8,128)S(1)}, f32[1,512,512]{2,1,0:T(8,128)S(1)}, u32[]{:S(2)}, u32[]{:S(2)}) collective-permute-start(f32[1,512,512]{2,1,0:T(8,128)S(1)} %fusion.35), channel_id=1, source_target_pairs={{0,1},{1,2},{2,3},{4,5},{5,6},{6,7},{8,9},{9,10},{10,11},{12,13},{... | collective-permute-start | bytes 3145736 | tf_op jit(solution)/shard_map/ppermute | solution.py:26
  117.9 27.2 %collective-permute-start.1 = (f32[1,512,512]{2,1,0:T(8,128)S(1)}, f32[1,512,512]{2,1,0:T(8,128)S(1)}, u32[]{:S(2)}, u32[]{:S(2)}) collective-permute-start(f32[1,512,512]{2,1,0:T(8,128)S(1)} %fusion.35), channel_id=1, source_target_pairs={{1,0},{2,1},{3,2},{5,4},{6,5},{7,6},{9,8},{10,9},{11,10},{13,12},{... | collective-permute-start | bytes 3145736 | tf_op jit(solution)/shard_map/ppermute | solution.py:29
  149.6 331.4 %all-reduce.6.cloned.1.call-start = ((), (), s32[]{:S(2)}) async-start(), calls=%async_computation.1 | async-start | bytes 524288 | tf_op jit(solution)/shard_map/psum | solution.py:75
  276.5 0.7 copy-start.3
  396.1 1.1 copy-start.4
Sparse Core Ops, SparseCore 0:
  10.5 103.3 all-gather.3
  149.7 101.3 all-reduce.3
  404.1 76.8 all-reduce.5
where the time goes:
time: 495 us; the launch traced here: 490 us
  waiting for transfers between devices  282 us (57%)
  other arithmetic  127 us (26%)
  blocking collectives  23.6 us (5%)
  local copies, waits for them, and re-layouts  17.8 us (4%)
  between operations  16.8 us (3%)
  matrix products  16.5 us (3%)
  starting transfers between devices  6.49 us (1%)
    psum x1, waiting for transfers between devices, body(): gram = lax.psum(local_gram, 'rx')  101 us
    another operation x14, other arithmetic, body(): factor = jnp.linalg.cholesky(gram)  82.9 us
    all_gather x1, waiting for transfers between devices, prefix_2(): gathered = jax.tree.map(lambda a: lax.all_gather(a, axis), part)  79.9 us
    psum x1, waiting for transfers between devices, body(): lax.psum(local_coords.astype(jnp.bfloat16), 'rx').astype(jnp.float32)  75.9 us
    another operation x3, other arithmetic, body(): ortho = jax.scipy.linalg.solve_triangular(factor, mixed.T, lower=True).T  40.4 us
    all_gather x1, blocking collectives, prefix_2(): gathered = jax.tree.map(lambda a: lax.all_gather(a, axis), part)  23.6 us
    ppermute x1, waiting for transfers between devices, with_halo(): lax.ppermute(lax.slice_in_dim(block, block.shape[dim] - width, None, axis...  21 us
    another operation x12, local copies, waits for them, and re-layouts  10.9 us
  transfers between devices with their start and end apart: 5, of which 5 were waited for; matrix products, arithmetic and copies ran while one was open for 0% of the time, Pallas kernels for 0%

commit v1 on v0

--- a/solution.py
+++ b/solution.py
@@ -63,7 +63,9 @@
         precision=lax.Precision.HIGHEST,
         preferred_element_type=jnp.float32,
     )
-    gram = lax.psum(local_gram, "rx")
+    gram = local_gram
+    for hop_ in (1, 2, 4):
+        gram = gram + lax.ppermute(gram, "rx", [(dev, dev ^ hop_) for dev in range(8)])
     factor = jnp.linalg.cholesky(gram)
     ortho = jax.scipy.linalg.solve_triangular(factor, mixed.T, lower=True).T
     local_coords = jnp.dot(

time: 495 us -> 539 us (1.089)
  waiting for transfers between devices: 282 us -> 315 us
  starting transfers between devices: 6.49 us -> 21.6 us
    ppermute x0 -> x3, waiting for transfers between devices: none -> 116 us  [body(): lax.ppermute(gram, 'rx', [(dev, dev ^ hop_) for dev in range(8)])]
    psum x1 -> x0, waiting for transfers between devices: 101 us -> none  [body(): gram = lax.psum(local_gram, 'rx')]
    psum x1, waiting for transfers between devices: 75.9 us -> 94.3 us  [body(): lax.psum(local_coords.astype(jnp.bfloat16), 'rx').astype(jnp.float32)]
    ppermute x0 -> x3, starting transfers between devices: none -> 15.6 us  [body(): lax.ppermute(gram, 'rx', [(dev, dev ^ hop_) for dev in range(8)])]
  transfers between devices with their start and end apart: 5 -> 7, of which waited for: 5 -> 7; matrix products, arithmetic and copies ran while one was open for 0% -> 0% of each run, Pallas kernels for 0% -> 0%
where the time goes in v1:
time: 539 us; the launch traced here: 533 us
  waiting for transfers between devices  315 us (58%)
  other arithmetic  123 us (23%)
  blocking collectives  23.6 us (4%)
  starting transfers between devices  21.6 us (4%)
  matrix products  17.4 us (3%)
  between operations  17.4 us (3%)
  local copies, waits for them, and re-layouts  15.9 us (3%)
    ppermute x3, waiting for transfers between devices, body(): lax.ppermute(gram, 'rx', [(dev, dev ^ hop_) for dev in range(8)])  116 us
    psum x1, waiting for transfers between devices, body(): lax.psum(local_coords.astype(jnp.bfloat16), 'rx').astype(jnp.float32)  94.3 us
    all_gather x1, waiting for transfers between devices, prefix_2(): gathered = jax.tree.map(lambda a: lax.all_gather(a, axis), part)  79.9 us
    another operation x14, other arithmetic, body(): factor = jnp.linalg.cholesky(gram)  78.7 us
    another operation x3, other arithmetic, body(): ortho = jax.scipy.linalg.solve_triangular(factor, mixed.T, lower=True).T  40.3 us
    all_gather x1, blocking collectives, prefix_2(): gathered = jax.tree.map(lambda a: lax.all_gather(a, axis), part)  23.6 us
    ppermute x1, waiting for transfers between devices, with_halo(): lax.ppermute(lax.slice_in_dim(block, block.shape[dim] - width, None, axis...  21 us
    ppermute x3, starting transfers between devices, body(): lax.ppermute(gram, 'rx', [(dev, dev ^ hop_) for dev in range(8)])  15.6 us
  transfers between devices with their start and end apart: 7, of which 7 were waited for; matrix products, arithmetic and copies ran while one was open for 0% of the time, Pallas kernels for 0%

profile of v1, /device:TPU:2, one launch (start us, length us, event | category | flops | bytes accessed | tf_op | source)
XLA Modules:
  0.0 533.5 jit_solution(14632874524393708154)
XLA Ops:
  7.2 0.9 copy-done
  8.1 2.3 fusion.16
  10.5 23.6 %all-gather = f32[16,1,512]{2,1,0:T(1,128)S(1)} all-gather(f32[1,1,512]{2,1,0:T(1,128)} %param.8), channel_id=2, replica_groups=mesh['rx'=8,'tm'=16,'bin'=4] {'tm'}, dimensions={0}, use_global_device_ids=true | all-gather | bytes 34816 | tf_op jit(solution)/shard_map/all_gather | solution.py:10
  34.1 79.9 %all-gather.4.cloned.1.call-done = f32[8192,512]{1,0:T(8,128)} async-done(((f32[512,512]{1,0:T(8,128)}), f32[8192,512]{1,0:T(8,128)}) %all-gather.4.cloned.1.call-update) | async-done | bytes 16777232 | tf_op jit(solution)/shard_map/all_gather | solution.py:10
  114.5 3.4 collective-permute-start
  117.9 2.5 collective-permute-start.1
  120.4 21.0 %collective-permute-done = f32[1,512,512]{2,1,0:T(8,128)S(1)} collective-permute-done((f32[1,512,512]{2,1,0:T(8,128)S(1)}, f32[1,512,512]{2,1,0:T(8,128)S(1)}, u32[]{:S(2)}, u32[]{:S(2)}) %collective-permute-start) | collective-permute-done | bytes 1048608 | tf_op jit(solution)/shard_map/ppermute | solution.py:26
  141.4 3.7 collective-permute-done.1
  145.1 1.6 bitcast_add_fusion.2
  146.7 1.9 fusion.45
  148.6 3.4 collective-permute-start.2
  152.0 24.1 %collective-permute-done.2 = f32[512,512]{0,1:T(8,128)S(1)} collective-permute-done((f32[512,512]{0,1:T(8,128)S(1)}, f32[512,512]{0,1:T(8,128)S(1)}, u32[]{:S(2)}, u32[]{:S(2)}) %collective-permute-start.2) | collective-permute-done | bytes 1048608 | tf_op jit(solution)/shard_map/ppermute | solution.py:68
  176.2 4.3 collective-permute-start.3
  180.6 45.7 %collective-permute-done.3 = f32[512,512]{0,1:T(8,128)S(1)} collective-permute-done((f32[512,512]{0,1:T(8,128)S(1)}, f32[512,512]{0,1:T(8,128)S(1)}, u32[]{:S(2)}, u32[]{:S(2)}) %collective-permute-start.3) | collective-permute-done | bytes 1048608 | tf_op jit(solution)/shard_map/ppermute | solution.py:68
  226.4 7.9 %collective-permute-start.4 = (f32[512,512]{0,1:T(8,128)S(1)}, f32[512,512]{0,1:T(8,128)}, u32[]{:S(2)}, u32[]{:S(2)}) collective-permute-start(f32[512,512]{0,1:T(8,128)S(1)} %add.82), channel_id=1, source_target_pairs={{0,256},{64,320},{128,384},{192,448},{256,0},{320,64},{384,128},{4... | collective-permute-start | bytes 3145736 | tf_op jit(solution)/shard_map/ppermute | solution.py:68
  234.3 45.9 %collective-permute-done.4 = f32[512,512]{0,1:T(8,128)} collective-permute-done((f32[512,512]{0,1:T(8,128)S(1)}, f32[512,512]{0,1:T(8,128)}, u32[]{:S(2)}, u32[]{:S(2)}) %collective-permute-start.4) | collective-permute-done | bytes 1048608 | tf_op jit(solution)/shard_map/ppermute | solution.py:68
  280.2 1.4 add.83
  282.2 1.0 copy-done.2
  283.2 11.7 %cholesky.103 = f32[128,128]{1,0:T(8,128)S(1)} custom-call(f32[128,128]{1,0:T(8,128)S(1)} %cholesky.263), custom_call_target="Cholesky" | custom-call | tf_op jit(solution)/shard_map/jit(cholesky)/cholesky | solution.py:69
  295.1 9.8 %custom-call.31 = f32[1,128,128]{1,2,0:T(8,128)S(1)} custom-call(f32[1,128,128]{2,1,0:T(8,128)S(1)} %get-tuple-element.81), custom_call_target="InvertDiagBlocksLowerTriangular" | custom-call | tf_op jit(solution)/shard_map/jit(cholesky)/cholesky | solution.py:69
  304.9 1.2 constant_dynamic-update-slice_fusion.3
  306.1 1.3 slice_subtract_fusion
  307.4 11.7 %cholesky.215 = f32[128,128]{1,0:T(8,128)S(1)} custom-call(f32[128,128]{1,0:T(8,128)S(1)} %cholesky.267), custom_call_target="Cholesky" | custom-call | tf_op jit(solution)/shard_map/jit(cholesky)/cholesky | solution.py:69
  319.1 10.0 %custom-call.32 = f32[1,128,128]{1,2,0:T(8,128)S(1)} custom-call(f32[1,128,128]{2,1,0:T(8,128)S(1)} %get-tuple-element.78), custom_call_target="InvertDiagBlocksLowerTriangular" | custom-call | tf_op jit(solution)/shard_map/jit(cholesky)/cholesky | solution.py:69
  329.4 1.3 slice_subtract_fusion.1
  330.7 11.7 %cholesky.236 = f32[128,128]{1,0:T(8,128)S(1)} custom-call(f32[128,128]{1,0:T(8,128)S(1)} %cholesky.272), custom_call_target="Cholesky" | custom-call | tf_op jit(solution)/shard_map/jit(cholesky)/cholesky | solution.py:69
  342.4 0.7 compare_reduce_fusion.1
  343.1 9.8 %custom-call.33 = f32[1,128,128]{1,2,0:T(8,128)S(1)} custom-call(f32[1,128,128]{2,1,0:T(8,128)S(1)} %get-tuple-element.75), custom_call_target="InvertDiagBlocksLowerTriangular" | custom-call | tf_op jit(solution)/shard_map/jit(cholesky)/cholesky | solution.py:69
  353.2 1.2 slice_subtract_fusion.2
  354.4 11.7 %cholesky.253 = f32[128,128]{1,0:T(8,128)S(1)} custom-call(f32[128,128]{1,0:T(8,128)S(1)} %slice_subtract_fusion.2), custom_call_target="Cholesky" | custom-call | tf_op jit(solution)/shard_map/jit(cholesky)/cholesky | solution.py:69
  366.4 0.7 compare_reduce_fusion
  367.1 0.7 compare_reduce_fusion.2
  370.5 10.6 %while.14 = (s32[]{:T(128)}, f32[512,512]{1,0:T(8,128)S(1)}, s32[4,2]{0,1:T(2,128)S(1)}, f32[4,128,128]{2,1,0:T(8,128)}, s32[]{:T(128)}) while((s32[]{:T(128)}, f32[512,512]{1,0:T(8,128)S(1)}, s32[4,2]{0,1:T(2,128)S(1)}, f32[4,128,128]{2,1,0:T(8,128)}, s32[]{:T(128)}) %tuple.49), condition=%wide.while_cond, body=%wide.while_body.sunk | while | flops 2 | bytes 132705 | solution.py:70
  370.5 0.6 fusion.54
  371.1 2.0 bitcast_dynamic-update-slice_fusion.2
  373.2 0.6 fusion.54
  373.8 2.0 bitcast_dynamic-update-slice_fusion.2
  376.4 2.0 bitcast_dynamic-update-slice_fusion.2
  379.1 2.0 bitcast_dynamic-update-slice_fusion.2
  381.1 40.1 %custom-call.34 = f32[4,128,128]{1,2,0:T(8,128)S(1)} custom-call(f32[4,128,128]{2,1,0:T(8,128)} %get-tuple-element.45), custom_call_target="InvertDiagBlocksLowerTriangular" | custom-call | tf_op jit(solution)/shard_map/jit(_solve_triangular)/triangular_solve | solution.py:70
  422.7 1.0 convolution_subtract_fusion
  423.7 1.3 fusion.29
  424.9 1.5 convolution_subtract_fusion.2
  426.4 1.3 fusion.28
  427.7 1.3 fusion
  429.2 1.0 copy.15
  430.2 94.3 %all-reduce.3.cloned.1.call-done = bf16[1,256,512]{1,2,0:T(8,128)(2,1)} async-done(((bf16[1,256,512]{1,2,0:T(8,128)(2,1)}), bf16[1,256,512]{1,2,0:T(8,128)(2,1)}) %all-reduce.3.cloned.1.call-update) | async-done | bytes 262160 | tf_op jit(solution)/shard_map/psum | solution.py:77
  524.5 1.9 copy.16
  (48 shorter events, 5.5 us)
Async XLA Ops:
  7.2 1.0 copy-start
  7.2 107.0 %copy-start.5 = (f32[1,1,512]{2,1,0:T(1,128)S(1)}, f32[1,1,512]{2,1,0:T(1,128)}, u32[]{:S(2)}) copy-start(f32[1,1,512]{2,1,0:T(1,128)} %param.8) | copy-start | bytes 6148
  7.2 107.0 %copy-start.3 = (bf16[1,512,512]{2,1,0:T(8,128)(2,1)S(1)}, bf16[1,512,512]{2,1,0:T(8,128)(2,1)}, u32[]{:S(2)}) copy-start(bf16[1,512,512]{2,1,0:T(8,128)(2,1)} %param.9) | copy-start | bytes 1572868
  7.2 106.8 %all-gather.4.cloned.1.call-start = ((), (), s32[]{:S(2)}) async-start(), calls=%async_computation.1 | async-start | bytes 17825792 | tf_op jit(solution)/shard_map/all_gather | solution.py:10
  10.4 103.8 %copy-start.1 = (f32[512,512]{1,0:T(8,128)S(1)}, f32[512,512]{1,0:T(8,128)}, u32[]{:S(2)}) copy-start(f32[512,512]{1,0:T(8,128)} %fusion.16) | copy-start | bytes 3145732
  10.4 514.1 %all-reduce.3.cloned.1.call-start = ((), (), s32[]{:S(2)}) async-start(), calls=%async_computation | async-start | bytes 524288 | tf_op jit(solution)/shard_map/psum | solution.py:77
  114.5 27.0 %collective-permute-start = (f32[1,512,512]{2,1,0:T(8,128)S(1)}, f32[1,512,512]{2,1,0:T(8,128)S(1)}, u32[]{:S(2)}, u32[]{:S(2)}) collective-permute-start(f32[1,512,512]{2,1,0:T(8,128)S(1)} %fusion.40), channel_id=1, source_target_pairs={{0,1},{1,2},{2,3},{4,5},{5,6},{6,7},{8,9},{9,10},{10,11},{12,13},{... | collective-permute-start | bytes 3145736 | tf_op jit(solution)/shard_map/ppermute | solution.py:26
  117.9 27.2 %collective-permute-start.1 = (f32[1,512,512]{2,1,0:T(8,128)S(1)}, f32[1,512,512]{2,1,0:T(8,128)S(1)}, u32[]{:S(2)}, u32[]{:S(2)}) collective-permute-start(f32[1,512,512]{2,1,0:T(8,128)S(1)} %fusion.40), channel_id=1, source_target_pairs={{1,0},{2,1},{3,2},{5,4},{6,5},{7,6},{9,8},{10,9},{11,10},{13,12},{... | collective-permute-start | bytes 3145736 | tf_op jit(solution)/shard_map/ppermute | solution.py:29
  148.6 27.5 %collective-permute-start.2 = (f32[512,512]{0,1:T(8,128)S(1)}, f32[512,512]{0,1:T(8,128)S(1)}, u32[]{:S(2)}, u32[]{:S(2)}) collective-permute-start(f32[512,512]{0,1:T(8,128)S(1)} %fusion.45), channel_id=1, source_target_pairs={{0,64},{64,0},{128,192},{192,128},{256,320},{320,256},{384,448},{4... | collective-permute-start | bytes 3145736 | tf_op jit(solution)/shard_map/ppermute | solution.py:68
  176.2 50.0 %collective-permute-start.3 = (f32[512,512]{0,1:T(8,128)S(1)}, f32[512,512]{0,1:T(8,128)S(1)}, u32[]{:S(2)}, u32[]{:S(2)}) collective-permute-start(f32[512,512]{0,1:T(8,128)S(1)} %add.81), channel_id=1, source_target_pairs={{0,128},{64,192},{128,0},{192,64},{256,384},{320,448},{384,256},{4... | collective-permute-start | bytes 3145736 | tf_op jit(solution)/shard_map/ppermute | solution.py:68
  226.4 53.7 %collective-permute-start.4 = (f32[512,512]{0,1:T(8,128)S(1)}, f32[512,512]{0,1:T(8,128)}, u32[]{:S(2)}, u32[]{:S(2)}) collective-permute-start(f32[512,512]{0,1:T(8,128)S(1)} %add.82), channel_id=1, source_target_pairs={{0,256},{64,320},{128,384},{192,448},{256,0},{320,64},{384,128},{4... | collective-permute-start | bytes 3145736 | tf_op jit(solution)/shard_map/ppermute | solution.py:68
  282.2 1.0 copy-start.2
  421.2 1.1 copy-start.4
Sparse Core Ops, SparseCore 0:
  10.5 103.3 all-gather.3
  429.2 95.3 all-reduce.2
